TPU v7x, 512 devices: a whole 4x4x16 slice. The times are simulated.
512 devices in a mesh: band: 32 (over x, z_lo), grid: 16 (over z_hi, y, core).
Axes of the slice: x: 4, y: 4, z: 16 (z_hi: 2, z_lo: 8; z = z_hi * 8 + z_lo), core: 2. Of those that a mesh axis runs over, the one named last changes fastest.
Arguments:
- trial_bands: float32 [64, 160, 32, 128], P('band', 'grid'), may hold values from -6 to 6
- potential: float32 [160, 32, 128], P('grid'), may hold values from -2 to 0
Outputs:
- filtered: float32 [64, 160, 32, 128], P('band', 'grid')
- projected: float32 [64, 64], P('band')
- residual_norms: float32 [64], P('band')
All inputs are finite; a program needn't handle non-finite values.
Results may differ from a plain program's by a relative error of at most 0.00016.
Values sent between devices are 32-bit elements; how exact they have to be, the bound alone decides.
No kernel may reach another device: no remote copies, remote signals or barrier semaphores. Data moves between devices by JAX's collectives and lax.ppermute only.
A program may use at most 64 MiB of HBM per device.

v0:
```python
import jax
import jax.numpy as jnp
from jax import lax
from jax.sharding import PartitionSpec as P

CENTER = 4.25
HALF_WIDTH = 3.75
LOWEST = -2.0
SIGMA_ONE = HALF_WIDTH / (LOWEST - CENTER)
FOUR_THIRDS = 4.0 / 3.0
TWELFTH = 1.0 / 12.0
filter_degree = 4


def padded_2(cells, sides, width):
    for axis, dim in sides:
        count = lax.axis_size(axis)
        head = lax.slice_in_dim(cells, 0, width, axis=dim)
        tail = lax.slice_in_dim(cells, cells.shape[dim] - width, cells.shape[dim], axis=dim)
        cells = jnp.concatenate(
            [
                lax.ppermute(tail, axis, [(i, (i + 1) % count) for i in range(count)]),
                cells,
                lax.ppermute(head, axis, [((i + 1) % count, i) for i in range(count)]),
            ],
            axis=dim,
        )
    return cells


def operate(field_in, potential):
    padded = padded_2(field_in, (("grid", 1),), 2)
    plane_count = field_in.shape[1]
    near_sum = padded[:, 1 : 1 + plane_count] + padded[:, 3 : 3 + plane_count]
    near_sum = near_sum + jnp.roll(field_in, 1, 2) + jnp.roll(field_in, -1, 2)
    near_sum = near_sum + jnp.roll(field_in, 1, 3) + jnp.roll(field_in, -1, 3)
    far_sum = padded[:, 0:plane_count] + padded[:, 4 : 4 + plane_count]
    far_sum = far_sum + jnp.roll(field_in, 2, 2) + jnp.roll(field_in, -2, 2)
    far_sum = far_sum + jnp.roll(field_in, 2, 3) + jnp.roll(field_in, -2, 3)
    kinetic = 0.5 * (7.5 * field_in - FOUR_THIRDS * near_sum + TWELFTH * far_sum)
    return kinetic + potential * field_in


def on_device(trial_bands, potential):
    sigma_now = SIGMA_ONE
    previous = trial_bands
    current = (operate(trial_bands, potential) - CENTER * trial_bands) * (SIGMA_ONE / HALF_WIDTH)
    for repeat_index in range(filter_degree - 1):
        sigma_next = 1.0 / (2.0 / SIGMA_ONE - sigma_now)
        following = (operate(current, potential) - CENTER * current) * (
            2.0 * sigma_next / HALF_WIDTH
        ) - sigma_now * sigma_next * previous
        previous, current, sigma_now = (current, following, sigma_next)
    applied = operate(current, potential)
    band_count = current.shape[0]
    band_devices = lax.axis_size("band")
    total_bands = band_count * band_devices
    cell_count = current.shape[1] * current.shape[2] * current.shape[3]
    cell_total = cell_count * lax.axis_size("grid")
    inverse_cells = 1.0 / cell_total
    first_band = lax.axis_index("band") * band_count
    both = jnp.stack(
        [current.reshape(band_count, cell_count), applied.reshape(band_count, cell_count)]
    ).reshape(2, band_count, band_devices, cell_count // band_devices)
    moved = lax.all_to_all(both, "band", 2, 1, tiled=True)
    bands_here = moved[0].reshape(total_bands, -1)
    image_here = moved[1].reshape(total_bands, -1)
    margin_part = jnp.dot(
        bands_here,
        bands_here.T,
        precision=lax.Precision.HIGHEST,
        preferred_element_type=jnp.float32,
    )
    image_part = jnp.dot(
        image_here,
        bands_here.T,
        precision=lax.Precision.HIGHEST,
        preferred_element_type=jnp.float32,
    )
    norm_part = jnp.sum(image_here * image_here, axis=1)
    packed = jnp.concatenate([margin_part.reshape(-1), image_part.reshape(-1), norm_part])
    packed = lax.psum(packed, ("band", "grid")) * inverse_cells
    square = total_bands * total_bands
    margin = packed[:square].reshape(total_bands, total_bands)
    subspace = packed[square : 2 * square].reshape(total_bands, total_bands)
    image_norms = packed[2 * square :]
    factor = jnp.linalg.cholesky(margin)
    coefficients = lax.linalg.triangular_solve(factor, subspace.T, left_side=True, lower=True)
    projected = lax.linalg.triangular_solve(factor, coefficients.T, left_side=True, lower=True)
    residual_norms = image_norms - jnp.sum(coefficients * coefficients, axis=0)
    projected_rows = lax.dynamic_slice_in_dim(projected, first_band, band_count, 0)
    residual_rows = lax.dynamic_slice_in_dim(residual_norms, first_band, band_count, 0)
    return (current, projected_rows, residual_rows)


def solution(mesh):
    in_specs = (P("band", "grid", None, None), P("grid", None, None))
    out_specs = (P("band", "grid", None, None), P("band", None), P("band"))
    return jax.shard_map(
        on_device, mesh=mesh, in_specs=in_specs, out_specs=out_specs, check_vma=False
    )
```

profile of v0, /device:TPU:1, one launch (start us, length us, event | category | flops | bytes accessed | tf_op | source)
XLA Modules:
  0.0 275.6 jit_solution(5035472801133282586)
XLA Ops:
  0.6 0.9 fusion.146
  1.5 4.6 %collective-permute-start = (f32[2,2,32,128]{3,2,1,0:T(8,128)S(1)}, f32[2,2,32,128]{3,2,1,0:T(8,128)S(1)}, u32[]{:S(2)}, u32[]{:S(2)}) collective-permute-start(f32[2,2,32,128]{3,2,1,0:T(8,128)S(1)} %get-tuple-element.91), channel_id=1, source_target_pairs={{0,1},{1,2},{2,3},{3,4},{4,5},{5,6},{6,7},{7,8},{8,9},{9,10},{10,1... | collective-permute-start | bytes 196616 | tf_op jit(solution)/shard_map/ppermute | solution.py:22
  6.1 6.2 %collective-permute-start.1 = (f32[2,2,32,128]{3,2,1,0:T(8,128)S(1)}, f32[2,2,32,128]{3,2,1,0:T(8,128)S(1)}, u32[]{:S(2)}, u32[]{:S(2)}) collective-permute-start(f32[2,2,32,128]{3,2,1,0:T(8,128)S(1)} %get-tuple-element.92), channel_id=1, source_target_pairs={{1,0},{2,1},{3,2},{4,3},{5,4},{6,5},{7,6},{8,7},{9,8},{10,9},{11,1... | collective-permute-start | bytes 196616 | tf_op jit(solution)/shard_map/ppermute | solution.py:24
  12.4 1.2 fusion.150
  16.7 1.9 collective-permute-start.2
  18.6 14.5 %collective-permute-start.3 = (f32[2,2,32,128]{3,2,1,0:T(8,128)S(1)}, f32[2,2,32,128]{3,2,1,0:T(8,128)S(1)}, u32[]{:S(2)}, u32[]{:S(2)}) collective-permute-start(f32[2,2,32,128]{3,2,1,0:T(8,128)S(1)} %get-tuple-element.80), channel_id=1, source_target_pairs={{1,0},{2,1},{3,2},{4,3},{5,4},{6,5},{7,6},{8,7},{9,8},{10,9},{11,1... | collective-permute-start | bytes 196616 | tf_op jit(solution)/shard_map/ppermute | solution.py:24
  33.1 0.8 collective-permute-done.3
  35.5 1.9 collective-permute-start.4
  37.4 15.5 %collective-permute-start.5 = (f32[2,2,32,128]{3,2,1,0:T(8,128)S(1)}, f32[2,2,32,128]{3,2,1,0:T(8,128)S(1)}, u32[]{:S(2)}, u32[]{:S(2)}) collective-permute-start(f32[2,2,32,128]{3,2,1,0:T(8,128)S(1)} %get-tuple-element.62), channel_id=1, source_target_pairs={{1,0},{2,1},{3,2},{4,3},{5,4},{6,5},{7,6},{8,7},{9,8},{10,9},{11,1... | collective-permute-start | bytes 196616 | tf_op jit(solution)/shard_map/ppermute | solution.py:24
  52.9 0.8 collective-permute-done.5
  55.2 1.9 collective-permute-start.6
  57.2 15.5 %collective-permute-start.7 = (f32[2,2,32,128]{3,2,1,0:T(8,128)S(1)}, f32[2,2,32,128]{3,2,1,0:T(8,128)S(1)}, u32[]{:S(2)}, u32[]{:S(2)}) collective-permute-start(f32[2,2,32,128]{3,2,1,0:T(8,128)S(1)} %get-tuple-element.44), channel_id=1, source_target_pairs={{1,0},{2,1},{3,2},{4,3},{5,4},{6,5},{7,6},{8,7},{9,8},{10,9},{11,1... | collective-permute-start | bytes 196616 | tf_op jit(solution)/shard_map/ppermute | solution.py:24
  74.8 0.9 fusion.111
  75.7 0.9 fusion.112
  77.3 1.9 collective-permute-start.8
  79.2 15.5 %collective-permute-start.9 = (f32[2,2,32,128]{3,2,1,0:T(8,128)}, f32[2,2,32,128]{3,2,1,0:T(8,128)}, u32[]{:S(2)}, u32[]{:S(2)}) collective-permute-start(f32[2,2,32,128]{3,2,1,0:T(8,128)} %get-tuple-element.26), channel_id=1, source_target_pairs={{1,0},{2,1},{3,2},{4,3},{5,4},{6,5},{7,6},{8,7},{9,8},{10,9},{11,1... | collective-permute-start | bytes 196616 | tf_op jit(solution)/shard_map/ppermute | solution.py:24
  96.9 2.5 fusion.10
  99.4 1.1 stack.8
  100.5 1.4 copy.10
  101.9 10.4 %all-to-all-start = ((f32[2,2,32,1280]{3,1,0,2:T(2,128)}), f32[2,2,32,1280]{3,1,0,2:T(2,128)S(1)}, u32[]{:S(2)}, u32[]{:S(2)}) async-start(f32[2,2,32,1280]{3,1,0,2:T(2,128)} %copy.10), calls=%async_computation | async-start | bytes 1310720 | tf_op jit(solution)/shard_map/all_to_all | solution.py:65
  112.3 22.4 %all-to-all-done = f32[2,2,32,1280]{3,1,0,2:T(2,128)S(1)} async-done(((f32[2,2,32,1280]{3,1,0,2:T(2,128)}), f32[2,2,32,1280]{3,1,0,2:T(2,128)S(1)}, u32[]{:S(2)}, u32[]{:S(2)}) %all-to-all-start) | async-done | bytes 655392 | tf_op jit(solution)/shard_map/all_to_all | solution.py:65
  136.5 125.1 %psum.7 = f32[8256]{0:T(1024)S(1)} all-reduce(f32[8256]{0:T(1024)S(1)} %pad_maximum_fusion.9), channel_id=1, replica_groups=mesh['band'=32,'grid'=16] {'band','grid'}, use_global_device_ids=true, to_apply=%region_1.2 | all-reduce | flops 8256 | bytes 66048 | tf_op jit(solution)/shard_map/psum | solution.py:82
  261.8 5.8 %cholesky.18 = f32[64,64]{1,0:T(8,128)S(1)} custom-call(f32[64,64]{1,0:T(8,128)S(1)} %fusion.103), custom_call_target="Cholesky" | custom-call | tf_op jit(solution)/shard_map/jit(cholesky)/cholesky | solution.py:87
  269.0 4.9 %custom-call.8 = f32[1,64,64]{1,2,0:T(8,128)S(1)} custom-call(f32[1,64,64]{2,1,0:T(8,128)S(1)} %fusion.96), custom_call_target="InvertDiagBlocksLowerTriangular" | custom-call | tf_op jit(solution)/shard_map/triangular_solve/custom-call.0 | solution.py:89
  (94 shorter events, 15.8 us)
Async XLA Ops:
  1.5 13.5 %collective-permute-start = (f32[2,2,32,128]{3,2,1,0:T(8,128)S(1)}, f32[2,2,32,128]{3,2,1,0:T(8,128)S(1)}, u32[]{:S(2)}, u32[]{:S(2)}) collective-permute-start(f32[2,2,32,128]{3,2,1,0:T(8,128)S(1)} %get-tuple-element.91), channel_id=1, source_target_pairs={{0,1},{1,2},{2,3},{3,4},{4,5},{5,6},{6,7},{7,8},{8,9},{9,10},{10,1... | collective-permute-start | bytes 196616 | tf_op jit(solution)/shard_map/ppermute | solution.py:22
  6.1 7.5 %copy-start.1 = (f32[2,10,32,128]{3,2,1,0:T(8,128)S(1)}, f32[2,10,32,128]{3,2,1,0:T(8,128)}, u32[]{:S(2)}) copy-start(f32[2,10,32,128]{3,2,1,0:T(8,128)} %param.4) | copy-start | bytes 983044
  6.1 9.0 %collective-permute-start.1 = (f32[2,2,32,128]{3,2,1,0:T(8,128)S(1)}, f32[2,2,32,128]{3,2,1,0:T(8,128)S(1)}, u32[]{:S(2)}, u32[]{:S(2)}) collective-permute-start(f32[2,2,32,128]{3,2,1,0:T(8,128)S(1)} %get-tuple-element.92), channel_id=1, source_target_pairs={{1,0},{2,1},{3,2},{4,3},{5,4},{6,5},{7,6},{8,7},{9,8},{10,9},{11,1... | collective-permute-start | bytes 196616 | tf_op jit(solution)/shard_map/ppermute | solution.py:24
  14.1 0.9 copy-start.2
  16.7 16.4 %collective-permute-start.2 = (f32[2,2,32,128]{3,2,1,0:T(8,128)S(1)}, f32[2,2,32,128]{3,2,1,0:T(8,128)S(1)}, u32[]{:S(2)}, u32[]{:S(2)}) collective-permute-start(f32[2,2,32,128]{3,2,1,0:T(8,128)S(1)} %get-tuple-element.79), channel_id=1, source_target_pairs={{0,1},{1,2},{2,3},{3,4},{4,5},{5,6},{6,7},{7,8},{8,9},{9,10},{10,1... | collective-permute-start | bytes 196616 | tf_op jit(solution)/shard_map/ppermute | solution.py:22
  18.6 15.4 %collective-permute-start.3 = (f32[2,2,32,128]{3,2,1,0:T(8,128)S(1)}, f32[2,2,32,128]{3,2,1,0:T(8,128)S(1)}, u32[]{:S(2)}, u32[]{:S(2)}) collective-permute-start(f32[2,2,32,128]{3,2,1,0:T(8,128)S(1)} %get-tuple-element.80), channel_id=1, source_target_pairs={{1,0},{2,1},{3,2},{4,3},{5,4},{6,5},{7,6},{8,7},{9,8},{10,9},{11,1... | collective-permute-start | bytes 196616 | tf_op jit(solution)/shard_map/ppermute | solution.py:24
  35.5 17.4 %collective-permute-start.4 = (f32[2,2,32,128]{3,2,1,0:T(8,128)S(1)}, f32[2,2,32,128]{3,2,1,0:T(8,128)S(1)}, u32[]{:S(2)}, u32[]{:S(2)}) collective-permute-start(f32[2,2,32,128]{3,2,1,0:T(8,128)S(1)} %get-tuple-element.61), channel_id=1, source_target_pairs={{0,1},{1,2},{2,3},{3,4},{4,5},{5,6},{6,7},{7,8},{8,9},{9,10},{10,1... | collective-permute-start | bytes 196616 | tf_op jit(solution)/shard_map/ppermute | solution.py:22
  37.4 16.4 %collective-permute-start.5 = (f32[2,2,32,128]{3,2,1,0:T(8,128)S(1)}, f32[2,2,32,128]{3,2,1,0:T(8,128)S(1)}, u32[]{:S(2)}, u32[]{:S(2)}) collective-permute-start(f32[2,2,32,128]{3,2,1,0:T(8,128)S(1)} %get-tuple-element.62), channel_id=1, source_target_pairs={{1,0},{2,1},{3,2},{4,3},{5,4},{6,5},{7,6},{8,7},{9,8},{10,9},{11,1... | collective-permute-start | bytes 196616 | tf_op jit(solution)/shard_map/ppermute | solution.py:24
  55.2 17.5 %collective-permute-start.6 = (f32[2,2,32,128]{3,2,1,0:T(8,128)S(1)}, f32[2,2,32,128]{3,2,1,0:T(8,128)S(1)}, u32[]{:S(2)}, u32[]{:S(2)}) collective-permute-start(f32[2,2,32,128]{3,2,1,0:T(8,128)S(1)} %get-tuple-element.43), channel_id=1, source_target_pairs={{0,1},{1,2},{2,3},{3,4},{4,5},{5,6},{6,7},{7,8},{8,9},{9,10},{10,1... | collective-permute-start | bytes 196616 | tf_op jit(solution)/shard_map/ppermute | solution.py:22
  57.2 16.4 %collective-permute-start.7 = (f32[2,2,32,128]{3,2,1,0:T(8,128)S(1)}, f32[2,2,32,128]{3,2,1,0:T(8,128)S(1)}, u32[]{:S(2)}, u32[]{:S(2)}) collective-permute-start(f32[2,2,32,128]{3,2,1,0:T(8,128)S(1)} %get-tuple-element.44), channel_id=1, source_target_pairs={{1,0},{2,1},{3,2},{4,3},{5,4},{6,5},{7,6},{8,7},{9,8},{10,9},{11,1... | collective-permute-start | bytes 196616 | tf_op jit(solution)/shard_map/ppermute | solution.py:24
  74.2 21.9 %copy-start = (f32[2,10,32,128]{3,2,1,0:T(8,128)}, f32[2,10,32,128]{3,2,1,0:T(8,128)S(1)}, u32[]{:S(2)}) copy-start(f32[2,10,32,128]{3,2,1,0:T(8,128)S(1)} %fusion.25) | copy-start | bytes 983044
  77.3 18.9 %collective-permute-start.8 = (f32[2,2,32,128]{3,2,1,0:T(8,128)}, f32[2,2,32,128]{3,2,1,0:T(8,128)S(1)}, u32[]{:S(2)}, u32[]{:S(2)}) collective-permute-start(f32[2,2,32,128]{3,2,1,0:T(8,128)} %get-tuple-element.25), channel_id=1, source_target_pairs={{0,1},{1,2},{2,3},{3,4},{4,5},{5,6},{6,7},{7,8},{8,9},{9,10},{10,1... | collective-permute-start | bytes 196616 | tf_op jit(solution)/shard_map/ppermute | solution.py:22
  79.2 16.9 %collective-permute-start.9 = (f32[2,2,32,128]{3,2,1,0:T(8,128)}, f32[2,2,32,128]{3,2,1,0:T(8,128)}, u32[]{:S(2)}, u32[]{:S(2)}) collective-permute-start(f32[2,2,32,128]{3,2,1,0:T(8,128)} %get-tuple-element.26), channel_id=1, source_target_pairs={{1,0},{2,1},{3,2},{4,3},{5,4},{6,5},{7,6},{8,7},{9,8},{10,9},{11,1... | collective-permute-start | bytes 196616 | tf_op jit(solution)/shard_map/ppermute | solution.py:24
  96.1 0.7 copy-start.4
  96.1 0.7 copy-start.5
  99.4 1.1 copy-start.3
  101.9 32.8 %all-to-all-start = ((f32[2,2,32,1280]{3,1,0,2:T(2,128)}), f32[2,2,32,1280]{3,1,0,2:T(2,128)S(1)}, u32[]{:S(2)}, u32[]{:S(2)}) async-start(f32[2,2,32,1280]{3,1,0,2:T(2,128)} %copy.10), calls=%async_computation | async-start | bytes 1310720 | tf_op jit(solution)/shard_map/all_to_all | solution.py:65
where the time goes:
time: 276 us
  blocking collectives  125 us (45%)
  starting transfers between devices  89.9 us (33%)
  waiting for transfers between devices  25 us (9%)
  other arithmetic  17.6 us (6%)
  local copies, waits for them, and re-layouts  15.7 us (6%)
    psum x1, blocking collectives, on_device(): packed = lax.psum(packed, ('band', 'grid')) * inverse_cells  125 us
    ppermute x5, starting transfers between devices, padded_2(): lax.ppermute(head, axis, [((i + 1) % count, i) for i in range(count)])  67.2 us
    all_to_all x1, waiting for transfers between devices, on_device(): moved = lax.all_to_all(both, 'band', 2, 1, tiled=True)  22.4 us
    ppermute x5, starting transfers between devices, padded_2(): lax.ppermute(tail, axis, [(i, (i + 1) % count) for i in range(count)])  12.3 us
    all_to_all x1, starting transfers between devices, on_device(): moved = lax.all_to_all(both, 'band', 2, 1, tiled=True)  10.4 us
    another operation x3, other arithmetic, on_device(): factor = jnp.linalg.cholesky(margin)  6.52 us
    another operation x2, other arithmetic, on_device(): lax.linalg.triangular_solve(factor, coefficients.T, left_side=True, lower...  5.55 us
  transfers between devices with their start and end apart: 11, of which 4 were waited for; matrix products, arithmetic and copies ran while one was open for 1% of the time, Pallas kernels for 0%

commit v1 on v0

--- a/solution.py
+++ b/solution.py
@@ -2,6 +2,7 @@
 import jax.numpy as jnp
 from jax import lax
 from jax.sharding import PartitionSpec as P
+from jax.lax import all_gather
 
 CENTER = 4.25
 HALF_WIDTH = 3.75
@@ -10,6 +11,10 @@
 FOUR_THIRDS = 4.0 / 3.0
 TWELFTH = 1.0 / 12.0
 filter_degree = 4
+
+
+def trace_loads_in(incoming_x, axis_name):
+    return jnp.sum(all_gather(incoming_x, axis_name), axis=0)
 
 
 def padded_2(cells, sides, width):
@@ -79,7 +84,7 @@
     )
     norm_part = jnp.sum(image_here * image_here, axis=1)
     packed = jnp.concatenate([margin_part.reshape(-1), image_part.reshape(-1), norm_part])
-    packed = lax.psum(packed, ("band", "grid")) * inverse_cells
+    packed = trace_loads_in(packed, ("band", "grid")) * inverse_cells
     square = total_bands * total_bands
     margin = packed[:square].reshape(total_bands, total_bands)
     subspace = packed[square : 2 * square].reshape(total_bands, total_bands)

time: 276 us -> 750 us (2.72)
  waiting for transfers between devices: 25 us -> 566 us
  blocking collectives: 125 us -> 0 us
  local copies, waits for them, and re-layouts: 15.7 us -> 47.8 us
  between operations: 1.13 us -> 14.5 us
  other arithmetic: 17.6 us -> 28.6 us
    unnamed x0 -> x2, waiting for transfers between devices: none -> 541 us
    psum x1 -> x0, blocking collectives: 125 us -> none  [on_device(): packed = lax.psum(packed, ('band', 'grid')) * inverse_cells]
    all_gather x0 -> x1, local copies, waits for them, and re-layouts: none -> 19.3 us  [trace_loads_in(): return jnp.sum(all_gather(incoming_x, axis_name), axis=0)]
  transfers between devices with their start and end apart: 11 -> 12, of which waited for: 4 -> 5; matrix products, arithmetic and copies ran while one was open for 1% -> 2% of each run, Pallas kernels for 0% -> 0%
where the time goes in v1:
time: 750 us; the launch traced here: 748 us
  waiting for transfers between devices  566 us (75%)
  starting transfers between devices  90 us (12%)
  local copies, waits for them, and re-layouts  47.8 us (6%)
  other arithmetic  28.6 us (4%)
  between operations  14.5 us (2%)
    unnamed x2, waiting for transfers between devices  541 us
    ppermute x5, starting transfers between devices, padded_2(): lax.ppermute(head, axis, [((i + 1) % count, i) for i in range(count)])  67.1 us
    all_to_all x1, waiting for transfers between devices, on_device(): moved = lax.all_to_all(both, 'band', 2, 1, tiled=True)  22.2 us
    all_gather x1, local copies, waits for them, and re-layouts, trace_loads_in(): return jnp.sum(all_gather(incoming_x, axis_name), axis=0)  19.3 us
  transfers between devices with their start and end apart: 12, of which 5 were waited for; matrix products, arithmetic and copies ran while one was open for 2% of the time, Pallas kernels for 0%

profile of v1, /device:TPU:1, one launch (start us, length us, event | category | flops | bytes accessed | tf_op | source)
XLA Modules:
  0.0 747.9 jit_solution(6072653588970547377)
XLA Ops:
  8.1 4.6 collective-permute-start
  12.7 6.1 collective-permute-start.1
  23.3 1.3 fusion.149
  24.6 1.2 fusion.145
  30.0 1.7 broadcast_multiply_fusion
  32.5 1.9 collective-permute-start.2
  34.5 14.5 %collective-permute-start.3 = (f32[2,2,32,128]{3,2,1,0:T(8,128)S(1)}, f32[2,2,32,128]{3,2,1,0:T(8,128)S(1)}, u32[]{:S(2)}, u32[]{:S(2)}) collective-permute-start(f32[2,2,32,128]{3,2,1,0:T(8,128)S(1)} %get-tuple-element.80), channel_id=1, source_target_pairs={{1,0},{2,1},{3,2},{4,3},{5,4},{6,5},{7,6},{8,7},{9,8},{10,9},{11,1... | collective-permute-start | bytes 196616 | tf_op jit(solution)/shard_map/ppermute | solution.py:29
  51.3 1.9 collective-permute-start.4
  53.3 15.5 %collective-permute-start.5 = (f32[2,2,32,128]{3,2,1,0:T(8,128)S(1)}, f32[2,2,32,128]{3,2,1,0:T(8,128)S(1)}, u32[]{:S(2)}, u32[]{:S(2)}) collective-permute-start(f32[2,2,32,128]{3,2,1,0:T(8,128)S(1)} %get-tuple-element.62), channel_id=1, source_target_pairs={{1,0},{2,1},{3,2},{4,3},{5,4},{6,5},{7,6},{8,7},{9,8},{10,9},{11,1... | collective-permute-start | bytes 196616 | tf_op jit(solution)/shard_map/ppermute | solution.py:29
  71.1 1.9 collective-permute-start.6
  73.0 15.5 %collective-permute-start.7 = (f32[2,2,32,128]{3,2,1,0:T(8,128)S(1)}, f32[2,2,32,128]{3,2,1,0:T(8,128)S(1)}, u32[]{:S(2)}, u32[]{:S(2)}) collective-permute-start(f32[2,2,32,128]{3,2,1,0:T(8,128)S(1)} %get-tuple-element.44), channel_id=1, source_target_pairs={{1,0},{2,1},{3,2},{4,3},{5,4},{6,5},{7,6},{8,7},{9,8},{10,9},{11,1... | collective-permute-start | bytes 196616 | tf_op jit(solution)/shard_map/ppermute | solution.py:29
  93.1 1.9 collective-permute-start.8
  95.1 15.5 %collective-permute-start.9 = (f32[2,2,32,128]{3,2,1,0:T(8,128)}, f32[2,2,32,128]{3,2,1,0:T(8,128)}, u32[]{:S(2)}, u32[]{:S(2)}) collective-permute-start(f32[2,2,32,128]{3,2,1,0:T(8,128)} %get-tuple-element.26), channel_id=1, source_target_pairs={{1,0},{2,1},{3,2},{4,3},{5,4},{6,5},{7,6},{8,7},{9,8},{10,9},{11,1... | collective-permute-start | bytes 196616 | tf_op jit(solution)/shard_map/ppermute | solution.py:29
  112.0 2.5 fusion.10
  116.6 1.4 copy.10
  118.0 10.4 %all-to-all-start = ((f32[2,2,32,1280]{3,1,0,2:T(2,128)}), f32[2,2,32,1280]{3,1,0,2:T(2,128)S(1)}, u32[]{:S(2)}, u32[]{:S(2)}) async-start(f32[2,2,32,1280]{3,1,0,2:T(2,128)} %copy.10), calls=%async_computation | async-start | bytes 1310720 | tf_op jit(solution)/shard_map/all_to_all | solution.py:70
  128.6 22.2 %all-to-all-done = f32[2,2,32,1280]{3,1,0,2:T(2,128)S(1)} async-done(((f32[2,2,32,1280]{3,1,0,2:T(2,128)}), f32[2,2,32,1280]{3,1,0,2:T(2,128)S(1)}, u32[]{:S(2)}, u32[]{:S(2)}) %all-to-all-start) | async-done | bytes 655392 | tf_op jit(solution)/shard_map/all_to_all | solution.py:70
  152.6 6.0 broadcast.74
  158.7 1.5 maximum_dynamic-update-slice_fusion
  160.2 540.9 %all-reduce.3.cloned.1.call-done = f32[4227072]{0:T(1024)} async-done(((f32[4227072]{0:T(1024)}), f32[4227072]{0:T(1024)}) %all-reduce.3.cloned.1.call-update) | async-done | bytes 16908304
  701.1 19.3 %reshape.49 = f32[512,8256]{1,0:T(8,128)} reshape(f32[4227072]{0:T(1024)} %all-reduce.3.cloned.1.call-done) | data formatting | bytes 33816576 | tf_op jit(solution)/shard_map/all_gather | solution.py:17
  720.4 6.6 reduce_sum.31
  727.2 5.8 cholesky.18
  734.4 4.9 custom-call.8
  (93 shorter events, 28.3 us)
Async XLA Ops:
  7.2 42.7 %copy-start.1 = (f32[2,10,32,128]{3,2,1,0:T(8,128)S(1)}, f32[2,10,32,128]{3,2,1,0:T(8,128)}, u32[]{:S(2)}) copy-start(f32[2,10,32,128]{3,2,1,0:T(8,128)} %param.4) | copy-start | bytes 983044
  8.1 20.8 %collective-permute-start = (f32[2,2,32,128]{3,2,1,0:T(8,128)S(1)}, f32[2,2,32,128]{3,2,1,0:T(8,128)S(1)}, u32[]{:S(2)}, u32[]{:S(2)}) collective-permute-start(f32[2,2,32,128]{3,2,1,0:T(8,128)S(1)} %get-tuple-element.91), channel_id=1, source_target_pairs={{0,1},{1,2},{2,3},{3,4},{4,5},{5,6},{6,7},{7,8},{8,9},{9,10},{10,1... | collective-permute-start | bytes 196616 | tf_op jit(solution)/shard_map/ppermute | solution.py:27
  12.7 17.3 %collective-permute-start.1 = (f32[2,2,32,128]{3,2,1,0:T(8,128)S(1)}, f32[2,2,32,128]{3,2,1,0:T(8,128)S(1)}, u32[]{:S(2)}, u32[]{:S(2)}) collective-permute-start(f32[2,2,32,128]{3,2,1,0:T(8,128)S(1)} %get-tuple-element.92), channel_id=1, source_target_pairs={{1,0},{2,1},{3,2},{4,3},{5,4},{6,5},{7,6},{8,7},{9,8},{10,9},{11,1... | collective-permute-start | bytes 196616 | tf_op jit(solution)/shard_map/ppermute | solution.py:29
  23.3 46.3 %copy-start.2 = (f32[10,32,128]{2,1,0:T(8,128)S(1)}, f32[10,32,128]{2,1,0:T(8,128)}, u32[]{:S(2)}) copy-start(f32[10,32,128]{2,1,0:T(8,128)} %param.5) | copy-start | bytes 491524
  32.5 16.4 %collective-permute-start.2 = (f32[2,2,32,128]{3,2,1,0:T(8,128)S(1)}, f32[2,2,32,128]{3,2,1,0:T(8,128)S(1)}, u32[]{:S(2)}, u32[]{:S(2)}) collective-permute-start(f32[2,2,32,128]{3,2,1,0:T(8,128)S(1)} %get-tuple-element.79), channel_id=1, source_target_pairs={{0,1},{1,2},{2,3},{3,4},{4,5},{5,6},{6,7},{7,8},{8,9},{9,10},{10,1... | collective-permute-start | bytes 196616 | tf_op jit(solution)/shard_map/ppermute | solution.py:27
  34.5 15.4 %collective-permute-start.3 = (f32[2,2,32,128]{3,2,1,0:T(8,128)S(1)}, f32[2,2,32,128]{3,2,1,0:T(8,128)S(1)}, u32[]{:S(2)}, u32[]{:S(2)}) collective-permute-start(f32[2,2,32,128]{3,2,1,0:T(8,128)S(1)} %get-tuple-element.80), channel_id=1, source_target_pairs={{1,0},{2,1},{3,2},{4,3},{5,4},{6,5},{7,6},{8,7},{9,8},{10,9},{11,1... | collective-permute-start | bytes 196616 | tf_op jit(solution)/shard_map/ppermute | solution.py:29
  51.3 17.4 %collective-permute-start.4 = (f32[2,2,32,128]{3,2,1,0:T(8,128)S(1)}, f32[2,2,32,128]{3,2,1,0:T(8,128)S(1)}, u32[]{:S(2)}, u32[]{:S(2)}) collective-permute-start(f32[2,2,32,128]{3,2,1,0:T(8,128)S(1)} %get-tuple-element.61), channel_id=1, source_target_pairs={{0,1},{1,2},{2,3},{3,4},{4,5},{5,6},{6,7},{7,8},{8,9},{9,10},{10,1... | collective-permute-start | bytes 196616 | tf_op jit(solution)/shard_map/ppermute | solution.py:27
  53.3 16.4 %collective-permute-start.5 = (f32[2,2,32,128]{3,2,1,0:T(8,128)S(1)}, f32[2,2,32,128]{3,2,1,0:T(8,128)S(1)}, u32[]{:S(2)}, u32[]{:S(2)}) collective-permute-start(f32[2,2,32,128]{3,2,1,0:T(8,128)S(1)} %get-tuple-element.62), channel_id=1, source_target_pairs={{1,0},{2,1},{3,2},{4,3},{5,4},{6,5},{7,6},{8,7},{9,8},{10,9},{11,1... | collective-permute-start | bytes 196616 | tf_op jit(solution)/shard_map/ppermute | solution.py:29
  71.1 17.5 %collective-permute-start.6 = (f32[2,2,32,128]{3,2,1,0:T(8,128)S(1)}, f32[2,2,32,128]{3,2,1,0:T(8,128)S(1)}, u32[]{:S(2)}, u32[]{:S(2)}) collective-permute-start(f32[2,2,32,128]{3,2,1,0:T(8,128)S(1)} %get-tuple-element.43), channel_id=1, source_target_pairs={{0,1},{1,2},{2,3},{3,4},{4,5},{5,6},{6,7},{7,8},{8,9},{9,10},{10,1... | collective-permute-start | bytes 196616 | tf_op jit(solution)/shard_map/ppermute | solution.py:27
  73.0 16.4 %collective-permute-start.7 = (f32[2,2,32,128]{3,2,1,0:T(8,128)S(1)}, f32[2,2,32,128]{3,2,1,0:T(8,128)S(1)}, u32[]{:S(2)}, u32[]{:S(2)}) collective-permute-start(f32[2,2,32,128]{3,2,1,0:T(8,128)S(1)} %get-tuple-element.44), channel_id=1, source_target_pairs={{1,0},{2,1},{3,2},{4,3},{5,4},{6,5},{7,6},{8,7},{9,8},{10,9},{11,1... | collective-permute-start | bytes 196616 | tf_op jit(solution)/shard_map/ppermute | solution.py:29
  90.1 68.6 %copy-start = (f32[2,10,32,128]{3,2,1,0:T(8,128)}, f32[2,10,32,128]{3,2,1,0:T(8,128)S(1)}, u32[]{:S(2)}) copy-start(f32[2,10,32,128]{3,2,1,0:T(8,128)S(1)} %fusion.25) | copy-start | bytes 983044
  93.1 18.9 %collective-permute-start.8 = (f32[2,2,32,128]{3,2,1,0:T(8,128)}, f32[2,2,32,128]{3,2,1,0:T(8,128)S(1)}, u32[]{:S(2)}, u32[]{:S(2)}) collective-permute-start(f32[2,2,32,128]{3,2,1,0:T(8,128)} %get-tuple-element.25), channel_id=1, source_target_pairs={{0,1},{1,2},{2,3},{3,4},{4,5},{5,6},{6,7},{7,8},{8,9},{9,10},{10,1... | collective-permute-start | bytes 196616 | tf_op jit(solution)/shard_map/ppermute | solution.py:27
  95.1 16.9 %collective-permute-start.9 = (f32[2,2,32,128]{3,2,1,0:T(8,128)}, f32[2,2,32,128]{3,2,1,0:T(8,128)}, u32[]{:S(2)}, u32[]{:S(2)}) collective-permute-start(f32[2,2,32,128]{3,2,1,0:T(8,128)} %get-tuple-element.26), channel_id=1, source_target_pairs={{1,0},{2,1},{3,2},{4,3},{5,4},{6,5},{7,6},{8,7},{9,8},{10,9},{11,1... | collective-permute-start | bytes 196616 | tf_op jit(solution)/shard_map/ppermute | solution.py:29
  118.0 32.8 %all-to-all-start = ((f32[2,2,32,1280]{3,1,0,2:T(2,128)}), f32[2,2,32,1280]{3,1,0,2:T(2,128)S(1)}, u32[]{:S(2)}, u32[]{:S(2)}) async-start(f32[2,2,32,1280]{3,1,0,2:T(2,128)} %copy.10), calls=%async_computation | async-start | bytes 1310720 | tf_op jit(solution)/shard_map/all_to_all | solution.py:70
  128.4 572.7 %all-reduce.3.cloned.1.call-start = ((), (), s32[]{:S(2)}) async-start(), calls=%async_computation.1 | async-start | bytes 33816576
Sparse Core Ops, SparseCore 0:
  160.3 540.7 all-reduce.2
